TPU v7x, 256 devices: a whole 4x4x8 slice. The times are simulated.
256 devices in a mesh: req: 32 (over x, y, core), tp: 8 (over z).
Axes of the slice: x: 4, y: 4, z: 8, core: 2. Of those that a mesh axis runs over, the one named last changes fastest.
Arguments:
- query: bfloat16 [768, 4096], P('req', 'tp'), may hold values from -102 to 102
- new_key: bfloat16 [768, 1024], P('req', 'tp'), may hold values from -6 to 6
- new_value: bfloat16 [768, 1024], P('req', 'tp'), may hold values from -6 to 6
- prefix_key: bfloat16 [64, 6144, 1024], P('req', None, 'tp'), may hold values from -6 to 6
- prefix_value: bfloat16 [64, 6144, 1024], P('req', None, 'tp'), may hold values from -6 to 6
- suffix_key: bfloat16 [768, 128, 1024], P('req', None, 'tp'), may hold values from -6 to 6
- suffix_value: bfloat16 [768, 128, 1024], P('req', None, 'tp'), may hold values from -6 to 6
- group_ids: int32 [768], replicated, may hold values from 0 to 63, as said below
- prompt_len: int32 [64], P('req'), may hold values from 768 to 6144, as said below
- suffix_len: int32 [768], replicated, may hold values from 1 to 128, as said below
- o_weight: bfloat16 [4096, 4096], P('tp'), may hold values from -0.09375 to 0.09375
- residual: bfloat16 [768, 4096], P('req'), may hold values from -0.29882812 to 0.29882812
- norm_gain: bfloat16 [4096], replicated, may hold values from 0.5 to 1.5
Outputs:
- hidden: bfloat16 [768, 4096], P('req')
- normed: bfloat16 [768, 4096], P('req')
Inputs may be any that keep to these rules, and one draw needn't show every extreme that they name: Request r belongs to group group_ids[r]; groups 2k to 2k + 1 at a time are held together (group // 2 names the holder). Among each aligned block of 24 requests, every holder that appears is named by exactly 2 of them. `prompt_len`: some group has exactly 6144. `suffix_len`: some request has exactly 128.
All inputs are finite; a program needn't handle non-finite values.
Results may differ from a plain program's by a relative error of at most 0.008.
Values may be sent and summed in bfloat16 or wider, within the bound.
No kernel may reach another device: no remote copies, remote signals or barrier semaphores. Data moves between devices by JAX's collectives and lax.ppermute only.
A program may use at most 64 MiB of HBM per device.

v0:
```python
import math
import jax
import jax.numpy as jnp
from jax import lax
from jax.sharding import PartitionSpec as P

HD = 128
WIN = 4096
SINKS = 4
FAR_BELOW = -1e30
NORM_EPS = 1e-06


def prefix_attend(
    rows_query, row_group, row_suffix, prefix_key, prefix_value, prompt_len, first_group, blocks
):
    row_count = rows_query.shape[0]
    groups_dev = prefix_key.shape[0]
    prompt_max = prefix_key.shape[1]
    kv_dev = prefix_key.shape[2] // HD
    heads_dev = rows_query.shape[1] // HD
    repeat = heads_dev // kv_dev
    block_len = min(512, prompt_max)
    score_scale = 1.0 / math.sqrt(HD)
    local_group = row_group - first_group
    owned = (local_group >= 0) & (local_group < groups_dev)
    member = local_group[:, None] == jnp.arange(groups_dev, dtype=jnp.int32)[None, :]
    row_prompt = jnp.sum(jnp.where(member, prompt_len[None, :], 0), axis=1)
    row_low = row_prompt + row_suffix - WIN + 1
    queries = rows_query.reshape(row_count, kv_dev, repeat, HD)

    def key_step(block_index, loop_state):
        running, weight_sum, weighted = loop_state
        key_start = block_index * block_len
        key_block = lax.dynamic_slice_in_dim(prefix_key, key_start, block_len, 1).reshape(
            groups_dev, block_len, kv_dev, HD
        )
        value_block = lax.dynamic_slice_in_dim(prefix_value, key_start, block_len, 1).reshape(
            groups_dev, block_len, kv_dev, HD
        )
        scores = (
            jnp.einsum("rkhd,gpkd->rkhgp", queries, key_block, preferred_element_type=jnp.float32)
            * score_scale
        )
        positions = key_start + jnp.arange(block_len, dtype=jnp.int32)
        inside = positions[None, :] < prompt_len[:, None]
        window = (positions[None, :] < SINKS) | (positions[None, :] >= row_low[:, None])
        usable = member[:, :, None] & inside[None, :, :] & window[:, None, :]
        usable = usable[:, None, None, :, :]
        masked = jnp.where(usable, scores, FAR_BELOW)
        updated = jnp.maximum(running, jnp.max(masked, axis=(3, 4)))
        weights = jnp.where(usable, jnp.exp(masked - updated[..., None, None]), 0.0)
        rescale = jnp.exp(running - updated)
        weight_sum = weight_sum * rescale + jnp.sum(weights, axis=(3, 4))
        rounded = weights.astype(jnp.bfloat16)
        weighted = weighted * rescale[..., None] + jnp.einsum(
            "rkhgp,gpkd->rkhd", rounded, value_block, preferred_element_type=jnp.float32
        )
        return (updated, weight_sum, weighted)

    initial = (
        jnp.full((row_count, kv_dev, repeat), FAR_BELOW, jnp.float32),
        jnp.zeros((row_count, kv_dev, repeat), jnp.float32),
        jnp.zeros((row_count, kv_dev, repeat, HD), jnp.float32),
    )
    running, weight_sum, weighted = lax.fori_loop(0, blocks, key_step, initial)
    bounded = jnp.maximum(weight_sum, 1.0)
    normalized = jnp.where(owned[:, None, None, None], weighted / bounded[..., None], 0.0).reshape(
        row_count, heads_dev * HD
    )
    log_total = jnp.where(owned[:, None, None], running + jnp.log(bounded), 0.0).reshape(
        row_count, heads_dev
    )
    return (normalized, log_total)


def body(
    query,
    new_key,
    new_value,
    prefix_key,
    prefix_value,
    suffix_key,
    suffix_value,
    group_ids,
    prompt_len,
    suffix_len,
    o_weight,
    residual,
    norm_gain,
):
    req_dev = query.shape[0]
    heads_dev = query.shape[1] // HD
    kv_dev = new_key.shape[1] // HD
    repeat = heads_dev // kv_dev
    groups_dev = prefix_key.shape[0]
    prompt_max = prefix_key.shape[1]
    suffix_max = suffix_key.shape[1]
    block_len = min(512, prompt_max)
    score_scale = 1.0 / math.sqrt(HD)
    places = lax.axis_size("req")
    device = lax.axis_index("req")
    first_group = device * groups_dev
    own_suffix = lax.dynamic_slice_in_dim(suffix_len, device * req_dev, req_dev)
    blocks = prompt_max // block_len
    capacity = max(2, req_dev // places)
    slot_total = places * capacity
    all_groups = group_ids.reshape(places, 1, req_dev)
    all_suffix = suffix_len.reshape(places, 1, req_dev)
    all_rows = (
        jnp.arange(places, dtype=jnp.int32)[:, None] * req_dev
        + jnp.arange(req_dev, dtype=jnp.int32)[None, :]
    ).reshape(places, 1, req_dev)
    is_mine = (group_ids // groups_dev).reshape(places, req_dev) == device
    slot_order = jnp.cumsum(is_mine.astype(jnp.int32), axis=1) - 1
    slot_pick = is_mine[:, None, :] & (
        slot_order[:, None, :] == jnp.arange(capacity, dtype=jnp.int32)[None, :, None]
    )
    filled = jnp.any(slot_pick, axis=2)
    slot_group = jnp.where(
        filled, jnp.sum(jnp.where(slot_pick, all_groups, 0), axis=2), -1
    ).reshape(slot_total)
    slot_suffix = jnp.sum(jnp.where(slot_pick, all_suffix, 0), axis=2).reshape(slot_total)
    slot_row = jnp.where(filled, jnp.sum(jnp.where(slot_pick, all_rows, 0), axis=2), -1).reshape(
        slot_total
    )
    every_query = lax.all_gather(query, "req", axis=0, tiled=True)
    pick_rows = slot_row[:, None] == jnp.arange(places * req_dev, dtype=jnp.int32)[None, :]
    compact = jnp.dot(
        pick_rows.astype(jnp.bfloat16), every_query, preferred_element_type=jnp.float32
    ).astype(jnp.bfloat16)
    part_out, part_log = prefix_attend(
        compact, slot_group, slot_suffix, prefix_key, prefix_value, prompt_len, first_group, blocks
    )
    spread_rows = pick_rows.T.astype(jnp.float32)
    spread_out = jnp.dot(spread_rows, part_out, precision=lax.Precision.HIGHEST)
    spread_log = jnp.dot(spread_rows, part_log, precision=lax.Precision.HIGHEST)
    prefix_out, prefix_log = (
        lax.psum_scatter(spread_out, "req", scatter_dimension=0, tiled=True),
        lax.psum_scatter(spread_log, "req", scatter_dimension=0, tiled=True),
    )
    queries = query.reshape(req_dev, kv_dev, repeat, HD)
    key_rows = suffix_key.reshape(req_dev, suffix_max, kv_dev, HD)
    value_rows = suffix_value.reshape(req_dev, suffix_max, kv_dev, HD)
    scores = (
        jnp.einsum("rkhd,rjkd->rkhj", queries, key_rows, preferred_element_type=jnp.float32)
        * score_scale
    )
    own_score = (
        jnp.einsum(
            "rkhd,rkd->rkh",
            queries,
            new_key.reshape(req_dev, kv_dev, HD),
            preferred_element_type=jnp.float32,
        )
        * score_scale
    )
    usable = (jnp.arange(suffix_max, dtype=jnp.int32)[None, :] < own_suffix[:, None])[
        :, None, None, :
    ]
    masked = jnp.where(usable, scores, FAR_BELOW)
    running = jnp.maximum(jnp.max(masked, axis=-1), own_score)
    weights = jnp.where(usable, jnp.exp(masked - running[..., None]), 0.0)
    own_weight = jnp.exp(own_score - running)
    weight_sum = jnp.sum(weights, axis=-1) + own_weight
    weighted = jnp.einsum(
        "rkhj,rjkd->rkhd",
        weights.astype(jnp.bfloat16),
        value_rows,
        preferred_element_type=jnp.float32,
    )
    own_rounded = own_weight.astype(jnp.bfloat16).astype(jnp.float32)
    weighted = weighted + own_rounded[..., None] * new_value.reshape(req_dev, kv_dev, 1, HD).astype(
        jnp.float32
    )
    local_out = weighted / weight_sum[..., None]
    local_log = running + jnp.log(weight_sum)
    prefix_out = prefix_out.reshape(req_dev, kv_dev, repeat, HD)
    prefix_log = prefix_log.reshape(req_dev, kv_dev, repeat)
    combined = jnp.logaddexp(prefix_log, local_log)
    attended = (
        prefix_out * jnp.exp(prefix_log - combined)[..., None]
        + local_out * jnp.exp(local_log - combined)[..., None]
    )
    attended = attended.reshape(req_dev, heads_dev * HD).astype(jnp.bfloat16)
    partial_value = jnp.dot(attended, o_weight, preferred_element_type=jnp.float32)
    proj = lax.psum(partial_value, "tp")
    summed = residual.astype(jnp.float32) + proj
    hidden = summed.astype(jnp.bfloat16)
    inverse = lax.rsqrt(jnp.mean(summed * summed, axis=-1, keepdims=True) + NORM_EPS)
    normed = (summed * inverse * norm_gain.astype(jnp.float32)[None, :]).astype(jnp.bfloat16)
    return (hidden, normed)


def solution(mesh):
    placed = (
        P("req", "tp"),
        P("req", "tp"),
        P("req", "tp"),
        P("req", None, "tp"),
        P("req", None, "tp"),
        P("req", None, "tp"),
        P("req", None, "tp"),
        P(),
        P("req"),
        P(),
        P("tp", None),
        P("req", None),
        P(),
    )
    return jax.shard_map(
        body,
        mesh=mesh,
        in_specs=placed,
        out_specs=(P("req", None), P("req", None)),
        check_vma=False,
    )
```

profile of v0, /device:TPU:2, one launch (start us, length us, event | category | flops | bytes accessed | tf_op | source)
XLA Modules:
  0.0 305.6 jit_solution(10688126659396240701)
XLA Ops:
  11.4 24.9 %all_gather.3 = bf16[768,512]{1,0:T(8,128)(2,1)S(1)} all-gather(bf16[24,512]{1,0:T(8,128)(2,1)} %param.15), channel_id=1, replica_groups=mesh['req'=32,'tp'=8] {'req'}, dimensions={0}, use_global_device_ids=true | all-gather | bytes 811008 | tf_op jit(solution)/shard_map/all_gather | solution.py:127
  36.8 50.0 %while.18 = (s32[]{:T(128)}, f32[64,1,4]{0,2,1:T(4,128)S(1)}, f32[64,1,4]{0,2,1:T(4,128)S(1)}, f32[64,1,4,128]{3,0,2,1:T(8,128)S(1)}, s32[2]{0:T(128)}, /*index=...) while((s32[]{:T(128)}, f32[64,1,4]{0,2,1:T(4,128)S(1)}, ...), condition=%wide.region_9.10_spmd.clone, body=%wide.region_6.9_spmd.clone.sunk | while | flops 136876160 | bytes 4351967 | solution.py:66
  37.8 1.4 fusion.83
  39.6 1.4 fusion.86
  42.0 1.4 fusion.83
  43.8 1.4 fusion.86
  47.9 1.4 fusion.86
  52.1 1.4 fusion.86
  56.3 1.4 fusion.86
  58.7 1.4 fusion.83
  60.5 1.4 fusion.86
  62.9 1.4 fusion.83
  64.6 1.4 fusion.86
  68.8 1.4 fusion.86
  73.0 1.4 fusion.86
  77.1 1.4 fusion.86
  81.3 1.4 fusion.86
  83.7 1.4 fusion.83
  85.5 1.4 fusion.86
  87.2 2.0 fusion.27
  91.6 109.0 %all-reduce = f32[768,4]{0,1:T(4,128)S(1)} all-reduce(f32[768,4]{0,1:T(4,128)S(1)} %fusion.26), channel_id=3, replica_groups=mesh['req'=32,'tp'=8] {'req'}, use_global_device_ids=true, to_apply=%region_11.12.clone | all-reduce | flops 3072 | bytes 24576
  203.2 3.6 %fusion.37 = f32[24,4096]{1,0:T(8,128)} fusion(bf16[512,4096]{1,0:T(8,128)(2,1)} %param.25, bf16[3,8,4,128]{3,2,1,0:T(4,128)(2,1)S(1)} %bitcast.93), kind=kOutput, calls=%fused_computation.57 | convolution fusion | flops 100663296 | bytes 4612096 | tf_op jit(solution)/shard_map/dot_general | solution.py:186
  206.8 88.9 %all-reduce.3.cloned.1.call-done = f32[24,4096]{1,0:T(8,128)} async-done(((f32[24,4096]{1,0:T(8,128)}), f32[24,4096]{1,0:T(8,128)}) %all-reduce.3.cloned.1.call-update) | async-done | bytes 393232 | tf_op jit(solution)/shard_map/psum | solution.py:187
  297.0 1.8 multiply_convert_fusion
  (201 shorter events, 35.8 us)
Async XLA Ops:
  7.2 193.8 %copy-start = (bf16[24,128,128]{2,1,0:T(8,128)(2,1)S(1)}, bf16[24,128,128]{2,1,0:T(8,128)(2,1)}, u32[]{:S(2)}) copy-start(bf16[24,128,128]{2,1,0:T(8,128)(2,1)} %param.20) | copy-start | bytes 2359300
  7.2 194.8 %reduce-scatter.3.cloned.1.call-start = ((), (), s32[]{:S(2)}) async-start(), calls=%async_computation.1 | async-start | bytes 1622016 | tf_op jit(solution)/shard_map/reduce_scatter | solution.py:139
  86.9 2.4 copy-start.2
  86.9 3.2 %copy-start.7 = (u32[256]{0:T(256)S(1)}, u32[256]{0:T(256)}, u32[]{:S(2)}) copy-start(u32[256]{0:T(256)} %constant.130) | copy-start | bytes 3076
  86.9 113.9 %copy-start.4 = (bf16[24,128]{1,0:T(8,128)(2,1)S(1)}, bf16[24,128]{1,0:T(8,128)(2,1)}, u32[]{:S(2)}) copy-start(bf16[24,128]{1,0:T(8,128)(2,1)} %param.17) | copy-start | bytes 18436
  86.9 113.9 %copy-start.6 = (bf16[24,128]{1,0:T(8,128)(2,1)S(1)}, bf16[24,128]{1,0:T(8,128)(2,1)}, u32[]{:S(2)}) copy-start(bf16[24,128]{1,0:T(8,128)(2,1)} %param.16) | copy-start | bytes 18436
  86.9 115.8 %copy-start.5 = (bf16[24,128,128]{2,1,0:T(8,128)(2,1)S(1)}, bf16[24,128,128]{2,1,0:T(8,128)(2,1)}, u32[]{:S(2)}) copy-start(bf16[24,128,128]{2,1,0:T(8,128)(2,1)} %param.21) | copy-start | bytes 2359300
  89.2 206.5 %all-reduce.3.cloned.1.call-start = ((), (), s32[]{:S(2)}) async-start(), calls=%async_computation.2 | async-start | bytes 786432 | tf_op jit(solution)/shard_map/psum | solution.py:187
  202.8 4.0 %copy-start.3 = (bf16[4096]{0:T(1024)(128)(2,1)S(1)}, bf16[4096]{0:T(1024)(128)(2,1)}, u32[]{:S(2)}) copy-start(bf16[4096]{0:T(1024)(128)(2,1)} %param.27) | copy-start | bytes 24580
  202.8 93.0 %copy-start.1 = (bf16[24,4096]{1,0:T(8,128)(2,1)S(1)}, bf16[24,4096]{1,0:T(8,128)(2,1)}, u32[]{:S(2)}) copy-start(bf16[24,4096]{1,0:T(8,128)(2,1)} %param.26) | copy-start | bytes 589828
Sparse Core Ops, SparseCore 0:
  89.4 86.8 reduce-scatter.2
  206.9 88.8 all-reduce.2
where the time goes:
time: 307 us; the launch traced here: 306 us
  blocking collectives  134 us (44%)
  waiting for transfers between devices  89 us (29%)
  matrix products  40.4 us (13%)
  other arithmetic  21.3 us (7%)
  between operations  15 us (5%)
  local copies, waits for them, and re-layouts  5.04 us (2%)
    unnamed x1, blocking collectives  109 us
    psum x1, waiting for transfers between devices, body(): proj = lax.psum(partial_value, 'tp')  88.9 us
    all_gather x1, blocking collectives, body(): every_query = lax.all_gather(query, 'req', axis=0, tiled=True)  24.9 us
    dot_general x12, matrix products, key_step(): jnp.einsum('rkhgp,gpkd->rkhd', rounded, value_block, preferred_element_ty...  16.8 us
    dot_general x12, matrix products, key_step(): jnp.einsum('rkhd,gpkd->rkhgp', queries, key_block, preferred_element_type...  16.3 us
    lt x12, other arithmetic, key_step(): inside = positions[None, :] < prompt_len[:, None]  8.77 us
  transfers between devices with their start and end apart: 2, of which 1 were waited for; matrix products, arithmetic and copies ran while one was open for 1% of the time, Pallas kernels for 0%

commit v1 on v0

--- a/solution.py
+++ b/solution.py
@@ -184,7 +184,7 @@
     )
     attended = attended.reshape(req_dev, heads_dev * HD).astype(jnp.bfloat16)
     partial_value = jnp.dot(attended, o_weight, preferred_element_type=jnp.float32)
-    proj = lax.psum(partial_value, "tp")
+    proj = jnp.sum(lax.all_gather(partial_value, "tp"), axis=0)
     summed = residual.astype(jnp.float32) + proj
     hidden = summed.astype(jnp.bfloat16)
     inverse = lax.rsqrt(jnp.mean(summed * summed, axis=-1, keepdims=True) + NORM_EPS)

time: 307 us -> 279 us (0.909)
  waiting for transfers between devices: 89 us -> 60.7 us
    psum x1 -> x0, waiting for transfers between devices: 88.9 us -> none  [body(): proj = lax.psum(partial_value, 'tp')]
    all_gather x0 -> x1, waiting for transfers between devices: none -> 60.7 us  [body(): proj = jnp.sum(lax.all_gather(partial_value, 'tp'), axis=0)]
where the time goes in v1:
time: 279 us; the launch traced here: 277 us
  blocking collectives  134 us (48%)
  waiting for transfers between devices  60.7 us (22%)
  matrix products  40.3 us (14%)
  other arithmetic  21.3 us (8%)
  between operations  15 us (5%)
  local copies, waits for them, and re-layouts  5.04 us (2%)
    unnamed x1, blocking collectives  109 us
    all_gather x1, waiting for transfers between devices, body(): proj = jnp.sum(lax.all_gather(partial_value, 'tp'), axis=0)  60.7 us
    all_gather x1, blocking collectives, body(): every_query = lax.all_gather(query, 'req', axis=0, tiled=True)  24.9 us
    dot_general x12, matrix products, key_step(): jnp.einsum('rkhgp,gpkd->rkhd', rounded, value_block, preferred_element_ty...  16.7 us
    dot_general x12, matrix products, key_step(): jnp.einsum('rkhd,gpkd->rkhgp', queries, key_block, preferred_element_type...  16.3 us
    lt x12, other arithmetic, key_step(): inside = positions[None, :] < prompt_len[:, None]  8.77 us
  transfers between devices with their start and end apart: 2, of which 1 were waited for; matrix products, arithmetic and copies ran while one was open for 1% of the time, Pallas kernels for 0%

profile of v1, /device:TPU:2, one launch (start us, length us, event | category | flops | bytes accessed | tf_op | source)
XLA Modules:
  0.0 277.4 jit_solution(13008412157565895615)
XLA Ops:
  11.6 24.9 %all_gather.9 = bf16[768,512]{1,0:T(8,128)(2,1)S(1)} all-gather(bf16[24,512]{1,0:T(8,128)(2,1)} %param.15), channel_id=1, replica_groups=mesh['req'=32,'tp'=8] {'req'}, dimensions={0}, use_global_device_ids=true | all-gather | bytes 811008 | tf_op jit(solution)/shard_map/all_gather | solution.py:127
  36.8 50.0 %while.18 = (s32[]{:T(128)}, f32[64,1,4]{0,2,1:T(4,128)S(1)}, f32[64,1,4]{0,2,1:T(4,128)S(1)}, f32[64,1,4,128]{3,0,2,1:T(8,128)S(1)}, s32[2]{0:T(128)}, /*index=...) while((s32[]{:T(128)}, f32[64,1,4]{0,2,1:T(4,128)S(1)}, ...), condition=%wide.region_9.10_spmd.clone, body=%wide.region_6.9_spmd.clone.sunk | while | flops 136876160 | bytes 4351959 | solution.py:66
  37.8 1.4 fusion.83
  39.2 1.4 fusion.86
  43.4 1.4 fusion.86
  46.2 1.4 fusion.83
  47.6 1.4 fusion.86
  51.7 1.4 fusion.86
  55.9 1.4 fusion.86
  58.7 1.4 fusion.83
  60.1 1.4 fusion.86
  64.2 1.4 fusion.86
  68.4 1.4 fusion.86
  71.2 1.4 fusion.83
  72.6 1.4 fusion.86
  76.7 1.4 fusion.86
  80.9 1.4 fusion.86
  83.7 1.4 fusion.83
  85.0 1.4 fusion.86
  87.1 2.0 fusion.27
  90.8 109.1 %all-reduce = f32[768,4]{0,1:T(4,128)S(1)} all-reduce(f32[768,4]{0,1:T(4,128)S(1)} %fusion.26), channel_id=4, replica_groups=mesh['req'=32,'tp'=8] {'req'}, use_global_device_ids=true, to_apply=%region_11.12.clone | all-reduce | flops 3072 | bytes 24576
  203.2 3.6 %fusion.37 = f32[24,4096]{1,0:T(8,128)} fusion(bf16[512,4096]{1,0:T(8,128)(2,1)} %param.25, bf16[3,8,4,128]{3,2,1,0:T(4,128)(2,1)S(1)} %bitcast.95), kind=kOutput, calls=%fused_computation.57 | convolution fusion | flops 100663296 | bytes 4612096 | tf_op jit(solution)/shard_map/dot_general | solution.py:186
  206.9 60.7 %all-gather.3.cloned.1.call-done = f32[192,4096]{1,0:T(8,128)} async-done(((f32[24,4096]{1,0:T(8,128)}), f32[192,4096]{1,0:T(8,128)}) %all-gather.3.cloned.1.call-update) | async-done | bytes 3145744 | tf_op jit(solution)/shard_map/all_gather | solution.py:187
  267.5 2.1 reduce_sum.81
  (202 shorter events, 35.5 us)
Async XLA Ops:
  7.2 193.8 %copy-start = (bf16[24,128,128]{2,1,0:T(8,128)(2,1)S(1)}, bf16[24,128,128]{2,1,0:T(8,128)(2,1)}, u32[]{:S(2)}) copy-start(bf16[24,128,128]{2,1,0:T(8,128)(2,1)} %param.20) | copy-start | bytes 2359300
  7.2 194.7 %reduce-scatter.3.cloned.1.call-start = ((), (), s32[]{:S(2)}) async-start(), calls=%async_computation.1 | async-start | bytes 1622016 | tf_op jit(solution)/shard_map/reduce_scatter | solution.py:139
  86.8 2.4 copy-start.2
  86.9 2.4 copy-start.7
  86.9 113.9 %copy-start.4 = (bf16[24,128]{1,0:T(8,128)(2,1)S(1)}, bf16[24,128]{1,0:T(8,128)(2,1)}, u32[]{:S(2)}) copy-start(bf16[24,128]{1,0:T(8,128)(2,1)} %param.17) | copy-start | bytes 18436
  86.9 114.0 %copy-start.6 = (bf16[24,128]{1,0:T(8,128)(2,1)S(1)}, bf16[24,128]{1,0:T(8,128)(2,1)}, u32[]{:S(2)}) copy-start(bf16[24,128]{1,0:T(8,128)(2,1)} %param.16) | copy-start | bytes 18436
  86.9 115.9 %copy-start.5 = (bf16[24,128,128]{2,1,0:T(8,128)(2,1)S(1)}, bf16[24,128,128]{2,1,0:T(8,128)(2,1)}, u32[]{:S(2)}) copy-start(bf16[24,128,128]{2,1,0:T(8,128)(2,1)} %param.21) | copy-start | bytes 2359300
  89.2 178.3 %all-gather.3.cloned.1.call-start = ((), (), s32[]{:S(2)}) async-start(), calls=%async_computation.2 | async-start | bytes 3538944 | tf_op jit(solution)/shard_map/all_gather | solution.py:187
  202.8 4.1 %copy-start.3 = (bf16[4096]{0:T(1024)(128)(2,1)S(1)}, bf16[4096]{0:T(1024)(128)(2,1)}, u32[]{:S(2)}) copy-start(bf16[4096]{0:T(1024)(128)(2,1)} %param.27) | copy-start | bytes 24580
  203.2 66.5 %copy-start.1 = (bf16[24,4096]{1,0:T(8,128)(2,1)S(1)}, bf16[24,4096]{1,0:T(8,128)(2,1)}, u32[]{:S(2)}) copy-start(bf16[24,4096]{1,0:T(8,128)(2,1)} %param.26) | copy-start | bytes 589828
Sparse Core Ops, SparseCore 0:
  89.3 86.8 reduce-scatter.2
  207.0 60.5 all-gather.2
